TPU v7x, 256 devices: a whole 4x4x8 slice. The times are simulated.
256 devices in a mesh: seq: 32 (over x_hi, z, core), tp: 8 (over y, x_lo).
Axes of the slice: x: 4 (x_hi: 2, x_lo: 2; x = x_hi * 2 + x_lo), y: 4, z: 8, core: 2. Of those that a mesh axis runs over, the one named last changes fastest.
Arguments:
- proj: bfloat16 [4096, 3, 8192], P('seq', None, 'tp'), may hold values from -6 to 6
- cotangent: bfloat16 [4096, 8192], P('seq', 'tp'), may hold values from -6 to 6
- out_weight: bfloat16 [8192, 8192], P('seq', 'tp'), may hold values from -0.125 to 0.125
- short_weight: float32 [7, 3, 8192], P(None, None, 'tp'), may hold values from -2 to 2
- long_filter: float32 [4096, 8192], P('seq', 'tp')
Outputs:
- grad_proj: bfloat16 [4096, 3, 8192], P('seq', None, 'tp')
- grad_short: float32 [7, 3, 8192], P(None, None, 'tp')
- grad_filter: float32 [4096, 8192], P('seq', 'tp')
All inputs are finite; a program needn't handle non-finite values.
Results may differ from a plain program's by a relative error of at most 0.025.
Values may be sent and summed in bfloat16 or wider, within the bound.
No kernel may reach another device: no remote copies, remote signals or barrier semaphores. Data moves between devices by JAX's collectives and lax.ppermute only.
A program may use at most 128 MiB of HBM per device.

v0:
```python
import math
import jax
import jax.numpy as jnp
from jax import lax
from jax.sharding import PartitionSpec as P

highest = lax.Precision.HIGHEST


def shifted(value, axis, by):
    devices = lax.axis_size(axis)
    pairs = [(i, i + by) for i in range(devices) if 0 <= i + by < devices]
    return lax.ppermute(value, axis, pairs)


def angle_tables(row_count, col_count, modulus):
    row_index = jnp.arange(row_count, dtype=jnp.int32)[:, None]
    col_index = jnp.arange(col_count, dtype=jnp.int32)[None, :]
    phase = (row_index * col_index % modulus).astype(jnp.float32) * (2.0 * math.pi / modulus)
    return (jnp.cos(phase), jnp.sin(phase))


def split_length(length):
    whole_len = 2 * length
    ceiling = 1 << whole_len.bit_length() // 2 - 1
    first_len = 2 * math.gcd(length, ceiling)
    return (first_len, whole_len // first_len)


def spectrum(columns):
    length, channels = columns.shape
    first_len, second_len = split_length(length)
    lower_half = first_len // 2
    whole_len = first_len * second_len
    values = columns.astype(jnp.float32).reshape(lower_half, second_len * channels)
    cos_first, sin_first = angle_tables(first_len, lower_half, first_len)
    real_one = jnp.dot(cos_first, values, precision=highest).reshape(
        first_len, second_len, channels
    )
    imag_one = -jnp.dot(sin_first, values, precision=highest).reshape(
        first_len, second_len, channels
    )
    twist_cos, twist_sin = angle_tables(first_len, second_len, whole_len)
    twist_cos = twist_cos[:, :, None]
    twist_sin = twist_sin[:, :, None]
    real_two = real_one * twist_cos + imag_one * twist_sin
    imag_two = imag_one * twist_cos - real_one * twist_sin
    cos_second, sin_second = angle_tables(second_len, second_len, second_len)
    real_out = jnp.einsum("amc,ml->alc", real_two, cos_second, precision=highest) + jnp.einsum(
        "amc,ml->alc", imag_two, sin_second, precision=highest
    )
    imag_out = jnp.einsum("amc,ml->alc", imag_two, cos_second, precision=highest) - jnp.einsum(
        "amc,ml->alc", real_two, sin_second, precision=highest
    )
    return (real_out, imag_out)


def signal(real_in, imag_in):
    first_len, second_len, channels = real_in.shape
    lower_half = first_len // 2
    whole_len = first_len * second_len
    cos_second, sin_second = angle_tables(second_len, second_len, second_len)
    real_one = jnp.einsum("alc,lm->amc", real_in, cos_second, precision=highest) - jnp.einsum(
        "alc,lm->amc", imag_in, sin_second, precision=highest
    )
    imag_one = jnp.einsum("alc,lm->amc", real_in, sin_second, precision=highest) + jnp.einsum(
        "alc,lm->amc", imag_in, cos_second, precision=highest
    )
    twist_cos, twist_sin = angle_tables(first_len, second_len, whole_len)
    twist_cos = twist_cos[:, :, None]
    twist_sin = twist_sin[:, :, None]
    real_two = real_one * twist_cos - imag_one * twist_sin
    imag_two = real_one * twist_sin + imag_one * twist_cos
    cos_first, sin_first = angle_tables(lower_half, first_len, first_len)
    merged = jnp.dot(
        cos_first, real_two.reshape(first_len, second_len * channels), precision=highest
    ) - jnp.dot(sin_first, imag_two.reshape(first_len, second_len * channels), precision=highest)
    return merged.reshape(lower_half * second_len, channels) / whole_len


def complex_product(left_real, left_imag, right_real, right_imag):
    return (
        left_real * right_real - left_imag * right_imag,
        left_real * right_imag + left_imag * right_real,
    )


def conj_product(left_real, left_imag, right_real, right_imag):
    return (
        left_real * right_real + left_imag * right_imag,
        left_imag * right_real - left_real * right_imag,
    )


def times_bf16(left_array, right_array):
    return (left_array.astype(jnp.float32) * right_array.astype(jnp.float32)).astype(jnp.bfloat16)


def body(proj, cotangent, out_weight, short_weight, long_filter):
    tok_rows = proj.shape[0]
    channels = proj.shape[2]
    taps_count = short_weight.shape[0]
    rim_rows = taps_count - 1
    partial_value = lax.dot_general(
        cotangent,
        lax.all_gather(out_weight, "seq", axis=0, tiled=True),
        (((1,), (1,)), ((), ())),
        preferred_element_type=jnp.float32,
    )
    grad_out = lax.psum_scatter(
        partial_value.astype(jnp.bfloat16), "tp", scatter_dimension=1, tiled=True
    )
    lower_rows = shifted(proj[tok_rows - rim_rows :], "seq", 1)
    extended = jnp.concatenate([lower_rows, proj], axis=0)
    primed = short_weight[0] * extended[rim_rows : rim_rows + tok_rows]
    for offset in range(1, taps_count):
        primed = (
            primed
            + short_weight[offset] * extended[rim_rows - offset : rim_rows - offset + tok_rows]
        )
    primed = primed.astype(jnp.bfloat16)
    query_conv = primed[:, 0]
    keys_conv = primed[:, 1]
    value_conv = primed[:, 2]
    gated_input = times_bf16(keys_conv, value_conv)
    filter_cols = lax.all_to_all(
        long_filter.astype(jnp.bfloat16), "seq", split_axis=1, concat_axis=0, tiled=True
    ).astype(long_filter.dtype)
    filter_real, filter_imag = spectrum(filter_cols)
    gated_cols = lax.all_to_all(gated_input, "seq", split_axis=1, concat_axis=0, tiled=True)
    gated_real, gated_imag = spectrum(gated_cols)
    conv_cols = signal(*complex_product(gated_real, gated_imag, filter_real, filter_imag)).astype(
        jnp.bfloat16
    )
    conv_out = lax.all_to_all(conv_cols, "seq", split_axis=0, concat_axis=1, tiled=True)
    grad_query = times_bf16(grad_out, conv_out)
    grad_conv = times_bf16(grad_out, query_conv)
    grad_cols = lax.all_to_all(grad_conv, "seq", split_axis=1, concat_axis=0, tiled=True)
    grad_real, grad_imag = spectrum(grad_cols)
    gated_grad_cols = signal(*conj_product(grad_real, grad_imag, filter_real, filter_imag)).astype(
        jnp.bfloat16
    )
    filter_grad_cols = signal(*conj_product(grad_real, grad_imag, gated_real, gated_imag))
    gated_grad = lax.all_to_all(gated_grad_cols, "seq", split_axis=0, concat_axis=1, tiled=True)
    grad_filter = lax.all_to_all(
        filter_grad_cols.astype(jnp.bfloat16), "seq", split_axis=0, concat_axis=1, tiled=True
    ).astype(filter_grad_cols.dtype)
    grad_keys = times_bf16(gated_grad, value_conv)
    grad_value = times_bf16(gated_grad, keys_conv)
    grad_primed = jnp.stack([grad_query, grad_keys, grad_value], axis=1)
    next_rows = shifted(grad_primed[:rim_rows], "seq", -1)
    trailing = jnp.concatenate([grad_primed, next_rows], axis=0)
    grad_sum = short_weight[0] * trailing[0:tok_rows]
    for offset in range(1, taps_count):
        grad_sum = grad_sum + short_weight[offset] * trailing[offset : offset + tok_rows]
    grad_proj = grad_sum.astype(jnp.bfloat16)
    grad_wide = grad_primed.astype(jnp.float32)
    local_short = jnp.stack(
        [
            jnp.sum(
                grad_wide
                * extended[rim_rows - offset : rim_rows - offset + tok_rows].astype(jnp.float32),
                axis=0,
            )
            for offset in range(taps_count)
        ]
    )
    short_shape = local_short.shape
    grad_short = lax.psum(local_short.reshape(-1, channels), "seq").reshape(short_shape)
    return (grad_proj, grad_short, grad_filter)


def solution(mesh):
    in_specs = (
        P("seq", None, "tp"),
        P("seq", "tp"),
        P("seq", "tp"),
        P(None, None, "tp"),
        P("seq", "tp"),
    )
    out_specs = (P("seq", None, "tp"), P(None, None, "tp"), P("seq", "tp"))
    return jax.shard_map(body, mesh=mesh, in_specs=in_specs, out_specs=out_specs, check_vma=False)
```

profile of v0, /device:TPU:2, one launch (start us, length us, event | category | flops | bytes accessed | tf_op | source)
XLA Modules:
  0.0 583.1 jit_solution(17212374280899392005)
XLA Ops:
  8.7 1.7 collective-permute-start
  10.5 1.9 copy.45
  12.4 11.3 %all-to-all-start.1 = ((bf16[128,32,32]{0,2,1:T(8,128)(2,1)}), bf16[128,32,32]{0,2,1:T(8,128)(2,1)S(1)}, u32[]{:S(2)}, u32[]{:S(2)}) async-start(bf16[128,32,32]{0,2,1:T(8,128)(2,1)} %bitcast.8), calls=%async_computation.2 | async-start | bytes 524288 | tf_op jit(solution)/shard_map/all_to_all | solution.py:126
  23.9 128.3 %all-gather.2.cloned.1.call-done = bf16[8192,1024]{1,0:T(8,128)(2,1)} async-done(((bf16[256,1024]{1,0:T(8,128)(2,1)}), bf16[8192,1024]{1,0:T(8,128)(2,1)}) %all-gather.2.cloned.1.call-update) | async-done | bytes 16777232 | tf_op jit(solution)/shard_map/all_gather | solution.py:106
  152.2 12.7 %convolution_convert_fusion = bf16[128,8192]{1,0:T(8,128)(2,1)} fusion(bf16[128,1024]{1,0:T(8,128)(2,1)S(1)} %copy-done, bf16[8192,1024]{1,0:T(8,128)(2,1)} %all-gather.2.cloned.1.call-done), kind=kOutput, calls=%fused_computation | convolution fusion | flops 2148532224 | bytes 19136512 | tf_op jit(solution)/shard_map/dot_general | solution.py:104
  166.1 1.5 fusion.12
  168.5 5.8 all-to-all-start
  178.8 2.1 convolution_subtract_fusion.7
  181.0 1.2 fusion.72
  182.1 2.2 convolution_add_fusion.4
  184.3 4.6 all-to-all-done
  192.2 1.6 fusion.71
  193.8 2.2 convolution_subtract_fusion.8
  196.0 22.9 %reduce-scatter.2.cloned.1.call-done = bf16[128,1024]{1,0:T(8,128)(2,1)} async-done(((bf16[128,8192]{1,0:T(8,128)(2,1)}), bf16[128,1024]{1,0:T(8,128)(2,1)}) %reduce-scatter.2.cloned.1.call-update) | async-done | bytes 262160 | tf_op jit(solution)/shard_map/reduce_scatter | solution.py:110
  220.8 9.2 %all-to-all-start.3 = ((bf16[128,32,32]{0,2,1:T(8,128)(2,1)}), bf16[128,32,32]{0,2,1:T(8,128)(2,1)S(1)}, u32[]{:S(2)}, u32[]{:S(2)}) async-start(bf16[128,32,32]{0,2,1:T(8,128)(2,1)} %bitcast.22), calls=%async_computation.4 | async-start | bytes 524288 | tf_op jit(solution)/shard_map/all_to_all | solution.py:138
  231.1 2.1 convolution_add_fusion.5
  233.3 11.4 %all-to-all-done.3 = bf16[128,32,32]{0,2,1:T(8,128)(2,1)S(1)} async-done(((bf16[128,32,32]{0,2,1:T(8,128)(2,1)}), bf16[128,32,32]{0,2,1:T(8,128)(2,1)S(1)}, u32[]{:S(2)}, u32[]{:S(2)}) %all-to-all-start.3) | async-done | bytes 262176 | tf_op jit(solution)/shard_map/all_to_all | solution.py:138
  248.0 1.2 fusion.75
  249.2 1.2 fusion.74
  250.4 1.2 convolution_subtract_fusion.5
  252.5 2.0 multiply_subtract_fusion.1
  254.6 1.3 fusion.35
  255.9 1.2 fusion.37
  258.2 1.2 fusion.49
  260.6 1.2 fusion.43
  261.7 1.2 fusion.32
  262.9 1.2 fusion.31
  265.3 1.2 fusion.29
  267.6 3.5 multiply_add_fusion
  271.7 1.6 copy.64
  273.9 1.4 fusion.172
  275.9 1.4 fusion.5
  279.1 4.0 all-to-all-start.2
  283.1 1.8 copy.59
  285.6 1.3 fusion.170
  286.9 1.4 fusion.4
  290.1 7.6 %all-to-all-done.2 = bf16[32,128,32]{1,2,0:T(8,128)(2,1)S(1)} async-done(((bf16[32,128,32]{1,2,0:T(8,128)(2,1)}), bf16[32,128,32]{1,2,0:T(8,128)(2,1)S(1)}, u32[]{:S(2)}, u32[]{:S(2)}) %all-to-all-start.2) | async-done | bytes 262176 | tf_op jit(solution)/shard_map/all_to_all | solution.py:135
  297.8 4.1 all-to-all-start.4
  301.9 2.6 fusion.168
  304.5 1.4 fusion.3
  307.9 8.4 %all-to-all-done.4 = bf16[32,128,32]{1,2,0:T(8,128)(2,1)S(1)} async-done(((bf16[32,128,32]{1,2,0:T(8,128)(2,1)}), bf16[32,128,32]{1,2,0:T(8,128)(2,1)S(1)}, u32[]{:S(2)}, u32[]{:S(2)}) %all-to-all-start.4) | async-done | bytes 262176 | tf_op jit(solution)/shard_map/all_to_all | solution.py:144
  316.3 3.9 all-to-all-start.5
  322.3 1.7 fusion.25
  324.0 1.3 collective-permute-start.1
  325.4 9.4 %all-to-all-done.5 = bf16[32,128,32]{1,2,0:T(8,128)(2,1)S(1)} async-done(((bf16[32,128,32]{1,2,0:T(8,128)(2,1)}), bf16[32,128,32]{1,2,0:T(8,128)(2,1)S(1)}, u32[]{:S(2)}, u32[]{:S(2)}) %all-to-all-start.5) | async-done | bytes 262176 | tf_op jit(solution)/shard_map/all_to_all | solution.py:145
  336.1 2.3 fusion.19
  338.4 236.1 %all-reduce.2.cloned.1.call-done = f32[7,3,1024]{2,1,0:T(4,128)} async-done(((f32[7,3,1024]{2,1,0:T(4,128)}), f32[7,3,1024]{2,1,0:T(4,128)}) %all-reduce.2.cloned.1.call-update) | async-done | bytes 86032 | tf_op jit(solution)/shard_map/psum | solution.py:169
  574.6 1.6 copy.67
  (113 shorter events, 34.8 us)
Async XLA Ops:
  7.2 145.0 %copy-start = (bf16[128,1024]{1,0:T(8,128)(2,1)S(1)}, bf16[128,1024]{1,0:T(8,128)(2,1)}, u32[]{:S(2)}) copy-start(bf16[128,1024]{1,0:T(8,128)(2,1)} %param.6) | copy-start | bytes 786436
  7.2 16.6 %copy-start.21 = (f32[7,3,1024]{2,0,1:T(8,128)S(1)}, f32[7,3,1024]{2,0,1:T(8,128)}, u32[]{:S(2)}) copy-start(f32[7,3,1024]{2,0,1:T(8,128)} %param.8) | copy-start | bytes 258052
  7.2 145.0 %all-gather.2.cloned.1.call-start = ((), (), s32[]{:S(2)}) async-start(), calls=%async_computation.7 | async-start | bytes 17301504 | tf_op jit(solution)/shard_map/all_gather | solution.py:106
  8.7 156.4 %collective-permute-start = (bf16[6,3,1024]{2,0,1:T(8,128)(2,1)S(1)}, bf16[6,3,1024]{2,0,1:T(8,128)(2,1)S(1)}, u32[]{:S(2)}, u32[]{:S(2)}) collective-permute-start(bf16[6,3,1024]{2,0,1:T(8,128)(2,1)S(1)} %slice.87), channel_id=1, source_target_pairs={{0,8},{8,16},{16,24},{24,32},{32,40},{40,48},{48,56},{56,64},{64,7... | collective-permute-start | bytes 110600 | tf_op jit(solution)/shard_map/ppermute | solution.py:13
  12.4 156.1 %all-to-all-start.1 = ((bf16[128,32,32]{0,2,1:T(8,128)(2,1)}), bf16[128,32,32]{0,2,1:T(8,128)(2,1)S(1)}, u32[]{:S(2)}, u32[]{:S(2)}) async-start(bf16[128,32,32]{0,2,1:T(8,128)(2,1)} %bitcast.8), calls=%async_computation.2 | async-start | bytes 524288 | tf_op jit(solution)/shard_map/all_to_all | solution.py:126
  23.7 195.2 %reduce-scatter.2.cloned.1.call-start = ((), (), s32[]{:S(2)}) async-start(), calls=%async_computation.8 | async-start | bytes 2359296 | tf_op jit(solution)/shard_map/reduce_scatter | solution.py:110
  164.9 1.2 copy-start.7
  165.0 3.5 copy-start.11
  165.0 3.5 copy-start.13
  165.0 3.5 copy-start.15
  165.0 3.5 copy-start.17
  165.2 3.3 copy-start.19
  168.5 20.3 %all-to-all-start = ((bf16[128,32,32]{0,2,1:T(8,128)(2,1)}), bf16[128,32,32]{0,2,1:T(8,128)(2,1)S(1)}, u32[]{:S(2)}, u32[]{:S(2)}) async-start(bf16[128,32,32]{0,2,1:T(8,128)(2,1)} %bitcast.2), calls=%async_computation.1 | async-start | bytes 524288 | tf_op jit(solution)/shard_map/all_to_all | solution.py:130
  220.8 23.9 %all-to-all-start.3 = ((bf16[128,32,32]{0,2,1:T(8,128)(2,1)}), bf16[128,32,32]{0,2,1:T(8,128)(2,1)S(1)}, u32[]{:S(2)}, u32[]{:S(2)}) async-start(bf16[128,32,32]{0,2,1:T(8,128)(2,1)} %bitcast.22), calls=%async_computation.4 | async-start | bytes 524288 | tf_op jit(solution)/shard_map/all_to_all | solution.py:138
  250.3 1.2 copy-start.2
  250.4 1.5 copy-start.3
  250.4 1.8 copy-start.4
  250.4 2.1 copy-start.5
  279.1 5.9 %copy-start.6 = (f32[128,64,32]{0,1,2:T(8,128)S(1)}, f32[128,64,32]{0,1,2:T(8,128)}, u32[]{:S(2)}) copy-start(f32[128,64,32]{0,1,2:T(8,128)} %get-tuple-element.48) | copy-start | bytes 3145732
  279.1 18.7 %all-to-all-start.2 = ((bf16[32,128,32]{1,2,0:T(8,128)(2,1)}), bf16[32,128,32]{1,2,0:T(8,128)(2,1)S(1)}, u32[]{:S(2)}, u32[]{:S(2)}) async-start(bf16[32,128,32]{1,2,0:T(8,128)(2,1)} %copy.52), calls=%async_computation.3 | async-start | bytes 524288 | tf_op jit(solution)/shard_map/all_to_all | solution.py:135
  297.8 18.5 %all-to-all-start.4 = ((bf16[32,128,32]{1,2,0:T(8,128)(2,1)}), bf16[32,128,32]{1,2,0:T(8,128)(2,1)S(1)}, u32[]{:S(2)}, u32[]{:S(2)}) async-start(bf16[32,128,32]{1,2,0:T(8,128)(2,1)} %copy.61), calls=%async_computation.5 | async-start | bytes 524288 | tf_op jit(solution)/shard_map/all_to_all | solution.py:144
  316.3 18.5 %all-to-all-start.5 = ((bf16[32,128,32]{1,2,0:T(8,128)(2,1)}), bf16[32,128,32]{1,2,0:T(8,128)(2,1)S(1)}, u32[]{:S(2)}, u32[]{:S(2)}) async-start(bf16[32,128,32]{1,2,0:T(8,128)(2,1)} %copy.66), calls=%async_computation.6 | async-start | bytes 524288 | tf_op jit(solution)/shard_map/all_to_all | solution.py:145
  320.2 1.0 copy-start.9
  320.2 254.4 %all-reduce.2.cloned.1.call-start = ((), (), s32[]{:S(2)}) async-start(), calls=%async_computation.9 | async-start | bytes 229376 | tf_op jit(solution)/shard_map/psum | solution.py:169
  321.1 1.1 copy-start.8
  324.0 11.9 %collective-permute-start.1 = (bf16[6,3,1024]{2,0,1:T(8,128)(2,1)S(1)}, bf16[6,3,1024]{2,0,1:T(8,128)(2,1)S(1)}, u32[]{:S(2)}, u32[]{:S(2)}) collective-permute-start(bf16[6,3,1024]{2,0,1:T(8,128)(2,1)S(1)} %slice.122), channel_id=1, source_target_pairs={{8,0},{16,8},{24,16},{32,24},{40,32},{48,40},{56,48},{64,56},{72,6... | collective-permute-start | bytes 110600 | tf_op jit(solution)/shard_map/ppermute | solution.py:13
  325.4 10.5 %copy-start.10 = (f32[7,3,1024]{2,1,0:T(4,128)}, f32[7,3,1024]{2,1,0:T(4,128)S(1)}, u32[]{:S(2)}) copy-start(f32[7,3,1024]{2,1,0:T(4,128)S(1)} %constant_dynamic-update-slice_fusion) | copy-start | bytes 258052
  334.9 1.2 copy-start.12
  334.9 1.2 copy-start.14
  334.9 1.2 copy-start.16
  334.9 1.2 copy-start.18
  334.9 1.2 copy-start.20
  336.1 240.0 %copy-start.1 = (bf16[128,1024]{1,0:T(8,128)(2,1)S(1)}, bf16[128,1024]{1,0:T(8,128)(2,1)}, u32[]{:S(2)}) copy-start(bf16[128,1024]{1,0:T(8,128)(2,1)} %param.6) | copy-start | bytes 786436
Sparse Core Ops, SparseCore 0:
  10.8 141.3 all-gather.1
  165.1 53.7 reduce-scatter.1
  336.1 238.4 all-reduce.1
where the time goes:
time: 589 us; the launch traced here: 583 us
  waiting for transfers between devices  429 us (73%)
  matrix products  62.1 us (11%)
  starting transfers between devices  41.5 us (7%)
  local copies, waits for them, and re-layouts  27.9 us (5%)
  between operations  15 us (3%)
  other arithmetic  7.24 us (1%)
    psum x1, waiting for transfers between devices, body(): lax.psum(local_short.reshape(-1, channels), 'seq').reshape(short_shape)  236 us
    all_gather x1, waiting for transfers between devices, body(): lax.all_gather(out_weight, 'seq', axis=0, tiled=True)  128 us
    reduce_scatter x1, waiting for transfers between devices, body(): lax.psum_scatter(partial_value.astype(jnp.bfloat16), 'tp', scatter_dimens...  22.9 us
    dot_general x1, matrix products, body(): lax.dot_general(cotangent, lax.all_gather(out_weight, 'seq', axis=0, tile...  12.7 us
  transfers between devices with their start and end apart: 11, of which 8 were waited for; matrix products, arithmetic and copies ran while one was open for 10% of the time, Pallas kernels for 0%

commit v1 on v0

--- a/solution.py
+++ b/solution.py
@@ -1,10 +1,21 @@
+import functools
 import math
 import jax
 import jax.numpy as jnp
 from jax import lax
 from jax.sharding import PartitionSpec as P
+from jax.lax import all_gather
 
 highest = lax.Precision.HIGHEST
+
+
+def open_teams(slab_in, shard_axis):
+    q_next = all_gather(slab_in, shard_axis)
+    carry_out = jnp.sum(q_next, 0)
+    return carry_out
+
+
+unite_the_sources_all = functools.partial(open_teams, shard_axis="seq")
 
 
 def shifted(value, axis, by):
@@ -166,7 +177,7 @@
         ]
     )
     short_shape = local_short.shape
-    grad_short = lax.psum(local_short.reshape(-1, channels), "seq").reshape(short_shape)
+    grad_short = unite_the_sources_all(local_short.reshape(-1, channels)).reshape(short_shape)
     return (grad_proj, grad_short, grad_filter)
 
 

time: 589 us -> 414 us (0.70)
  waiting for transfers between devices: 429 us -> 249 us
    psum x1 -> x0, waiting for transfers between devices: 236 us -> none  [body(): lax.psum(local_short.reshape(-1, channels), 'seq').reshape(short_shape)]
    all_gather x0 -> x1, waiting for transfers between devices: none -> 47.5 us  [open_teams(): q_next = all_gather(slab_in, shard_axis)]
  transfers between devices with their start and end apart: 11 -> 11, of which waited for: 8 -> 8; matrix products, arithmetic and copies ran while one was open for 10% -> 14% of each run, Pallas kernels for 0% -> 0%
where the time goes in v1:
time: 414 us; the launch traced here: 406 us
  waiting for transfers between devices  249 us (60%)
  matrix products  62.2 us (15%)
  starting transfers between devices  41.2 us (10%)
  local copies, waits for them, and re-layouts  29.2 us (7%)
  between operations  14.9 us (4%)
  other arithmetic  9.58 us (2%)
    all_gather x1, waiting for transfers between devices, body(): lax.all_gather(out_weight, 'seq', axis=0, tiled=True)  128 us
    all_gather x1, waiting for transfers between devices, open_teams(): q_next = all_gather(slab_in, shard_axis)  47.5 us
    reduce_scatter x1, waiting for transfers between devices, body(): lax.psum_scatter(partial_value.astype(jnp.bfloat16), 'tp', scatter_dimens...  21.1 us
    all_to_all x1, waiting for transfers between devices, body(): lax.all_to_all(filter_grad_cols.astype(jnp.bfloat16), 'seq', split_axis=0...  14 us
    all_to_all x1, waiting for transfers between devices, body(): lax.all_to_all(gated_grad_cols, 'seq', split_axis=0, concat_axis=1, tiled...  13.5 us
    dot_general x1, matrix products, body(): lax.dot_general(cotangent, lax.all_gather(out_weight, 'seq', axis=0, tile...  12.7 us
    all_to_all x1, starting transfers between devices, body(): lax.all_to_all(long_filter.astype(jnp.bfloat16), 'seq', split_axis=1, con...  11.3 us
    all_to_all x1, waiting for transfers between devices, body(): lax.all_to_all(grad_conv, 'seq', split_axis=1, concat_axis=0, tiled=True)  11.3 us
  transfers between devices with their start and end apart: 11, of which 8 were waited for; matrix products, arithmetic and copies ran while one was open for 14% of the time, Pallas kernels for 0%

profile of v1, /device:TPU:2, one launch (start us, length us, event | category | flops | bytes accessed | tf_op | source)
XLA Modules:
  0.0 405.7 jit_solution(17451014721823698917)
XLA Ops:
  8.7 1.7 collective-permute-start
  10.5 1.9 copy.45
  12.4 11.3 %all-to-all-start.1 = ((bf16[128,32,32]{0,2,1:T(8,128)(2,1)}), bf16[128,32,32]{0,2,1:T(8,128)(2,1)S(1)}, u32[]{:S(2)}, u32[]{:S(2)}) async-start(bf16[128,32,32]{0,2,1:T(8,128)(2,1)} %bitcast.8), calls=%async_computation.2 | async-start | bytes 524288 | tf_op jit(solution)/shard_map/all_to_all | solution.py:137
  23.9 128.3 %all-gather.3.cloned.1.call-done = bf16[8192,1024]{1,0:T(8,128)(2,1)} async-done(((bf16[256,1024]{1,0:T(8,128)(2,1)}), bf16[8192,1024]{1,0:T(8,128)(2,1)}) %all-gather.3.cloned.1.call-update) | async-done | bytes 16777232 | tf_op jit(solution)/shard_map/all_gather | solution.py:117
  152.2 12.7 %convolution_convert_fusion = bf16[128,8192]{1,0:T(8,128)(2,1)} fusion(bf16[128,1024]{1,0:T(8,128)(2,1)S(1)} %copy-done, bf16[8192,1024]{1,0:T(8,128)(2,1)} %all-gather.3.cloned.1.call-done), kind=kOutput, calls=%fused_computation | convolution fusion | flops 2148532224 | bytes 19136512 | tf_op jit(solution)/shard_map/dot_general | solution.py:115
  166.1 1.5 fusion.12
  168.5 5.8 %all-to-all-start = ((bf16[128,32,32]{0,2,1:T(8,128)(2,1)}), bf16[128,32,32]{0,2,1:T(8,128)(2,1)S(1)}, u32[]{:S(2)}, u32[]{:S(2)}) async-start(bf16[128,32,32]{0,2,1:T(8,128)(2,1)} %bitcast.2), calls=%async_computation.1 | async-start | bytes 524288 | tf_op jit(solution)/shard_map/all_to_all | solution.py:141
  177.6 1.2 fusion.73
  178.8 2.1 convolution_subtract_fusion.7
  181.0 1.2 fusion.72
  182.1 2.1 convolution_add_fusion.4
  184.3 4.5 %all-to-all-done = bf16[128,32,32]{0,2,1:T(8,128)(2,1)S(1)} async-done(((bf16[128,32,32]{0,2,1:T(8,128)(2,1)}), bf16[128,32,32]{0,2,1:T(8,128)(2,1)S(1)}, u32[]{:S(2)}, u32[]{:S(2)}) %all-to-all-start) | async-done | bytes 262176 | tf_op jit(solution)/shard_map/all_to_all | solution.py:141
  192.2 1.8 fusion.68
  194.0 1.6 fusion.71
  195.6 2.2 convolution_subtract_fusion.8
  197.8 21.1 %reduce-scatter.2.cloned.1.call-done = bf16[128,1024]{1,0:T(8,128)(2,1)} async-done(((bf16[128,8192]{1,0:T(8,128)(2,1)}), bf16[128,1024]{1,0:T(8,128)(2,1)}) %reduce-scatter.2.cloned.1.call-update) | async-done | bytes 262160 | tf_op jit(solution)/shard_map/reduce_scatter | solution.py:121
  220.8 9.2 %all-to-all-start.3 = ((bf16[128,32,32]{0,2,1:T(8,128)(2,1)}), bf16[128,32,32]{0,2,1:T(8,128)(2,1)S(1)}, u32[]{:S(2)}, u32[]{:S(2)}) async-start(bf16[128,32,32]{0,2,1:T(8,128)(2,1)} %bitcast.204), calls=%async_computation.4 | async-start | bytes 524288 | tf_op jit(solution)/shard_map/all_to_all | solution.py:149
  230.0 1.2 fusion.70
  231.2 2.2 convolution_add_fusion.5
  233.3 11.3 %all-to-all-done.3 = bf16[128,32,32]{0,2,1:T(8,128)(2,1)S(1)} async-done(((bf16[128,32,32]{0,2,1:T(8,128)(2,1)}), bf16[128,32,32]{0,2,1:T(8,128)(2,1)S(1)}, u32[]{:S(2)}, u32[]{:S(2)}) %all-to-all-start.3) | async-done | bytes 262176 | tf_op jit(solution)/shard_map/all_to_all | solution.py:149
  248.0 1.2 fusion.75
  252.5 2.0 multiply_subtract_fusion.1
  254.6 1.3 fusion.35
  255.9 1.2 fusion.37
  260.6 1.2 fusion.43
  261.7 1.2 fusion.32
  262.9 1.2 fusion.31
  265.3 1.2 fusion.29
  267.6 3.6 multiply_add_fusion
  271.8 1.4 fusion.172
  273.8 1.4 fusion.5
  277.0 4.0 all-to-all-start.2
  281.0 1.8 copy.59
  283.5 1.4 fusion.170
  284.9 1.4 fusion.4
  288.1 7.6 %all-to-all-done.2 = bf16[32,128,32]{1,2,0:T(8,128)(2,1)S(1)} async-done(((bf16[32,128,32]{1,2,0:T(8,128)(2,1)}), bf16[32,128,32]{1,2,0:T(8,128)(2,1)S(1)}, u32[]{:S(2)}, u32[]{:S(2)}) %all-to-all-start.2) | async-done | bytes 262176 | tf_op jit(solution)/shard_map/all_to_all | solution.py:146
  295.7 3.9 all-to-all-start.4
  300.7 13.5 %all-to-all-done.4 = bf16[32,128,32]{1,2,0:T(8,128)(2,1)S(1)} async-done(((bf16[32,128,32]{1,2,0:T(8,128)(2,1)}), bf16[32,128,32]{1,2,0:T(8,128)(2,1)S(1)}, u32[]{:S(2)}, u32[]{:S(2)}) %all-to-all-start.4) | async-done | bytes 262176 | tf_op jit(solution)/shard_map/all_to_all | solution.py:155
  315.8 2.0 fusion.25
  318.6 1.8 copy.65
  321.1 1.3 fusion.168
  322.4 1.4 fusion.3
  325.6 3.9 all-to-all-start.5
  329.6 1.3 collective-permute-start.1
  330.9 14.0 %all-to-all-done.5 = bf16[32,128,32]{1,2,0:T(8,128)(2,1)S(1)} async-done(((bf16[32,128,32]{1,2,0:T(8,128)(2,1)}), bf16[32,128,32]{1,2,0:T(8,128)(2,1)S(1)}, u32[]{:S(2)}, u32[]{:S(2)}) %all-to-all-start.5) | async-done | bytes 262176 | tf_op jit(solution)/shard_map/all_to_all | solution.py:156
  346.1 2.3 fusion.19
  348.4 47.5 %all-gather.5.cloned.1.call-done = f32[32,21,1024]{2,1,0:T(8,128)} async-done(((f32[1,21,1024]{2,1,0:T(8,128)}), f32[32,21,1024]{2,1,0:T(8,128)}) %all-gather.5.cloned.1.call-update) | async-done | bytes 2752528 | tf_op jit(solution)/shard_map/all_gather | solution.py:13
  395.9 2.1 reduce_sum.79
  (102 shorter events, 37.9 us)
Async XLA Ops:
  7.2 145.0 %copy-start = (bf16[128,1024]{1,0:T(8,128)(2,1)S(1)}, bf16[128,1024]{1,0:T(8,128)(2,1)}, u32[]{:S(2)}) copy-start(bf16[128,1024]{1,0:T(8,128)(2,1)} %param.6) | copy-start | bytes 786436
  7.2 16.6 %copy-start.14 = (f32[7,3,1024]{2,0,1:T(8,128)S(1)}, f32[7,3,1024]{2,0,1:T(8,128)}, u32[]{:S(2)}) copy-start(f32[7,3,1024]{2,0,1:T(8,128)} %param.8) | copy-start | bytes 258052
  7.2 145.0 %all-gather.3.cloned.1.call-start = ((), (), s32[]{:S(2)}) async-start(), calls=%async_computation.7 | async-start | bytes 17301504 | tf_op jit(solution)/shard_map/all_gather | solution.py:117
  8.7 156.4 %collective-permute-start = (bf16[6,3,1024]{2,0,1:T(8,128)(2,1)S(1)}, bf16[6,3,1024]{2,0,1:T(8,128)(2,1)S(1)}, u32[]{:S(2)}, u32[]{:S(2)}) collective-permute-start(bf16[6,3,1024]{2,0,1:T(8,128)(2,1)S(1)} %slice.87), channel_id=1, source_target_pairs={{0,8},{8,16},{16,24},{24,32},{32,40},{40,48},{48,56},{56,64},{64,7... | collective-permute-start | bytes 110600 | tf_op jit(solution)/shard_map/ppermute | solution.py:24
  12.4 156.1 %all-to-all-start.1 = ((bf16[128,32,32]{0,2,1:T(8,128)(2,1)}), bf16[128,32,32]{0,2,1:T(8,128)(2,1)S(1)}, u32[]{:S(2)}, u32[]{:S(2)}) async-start(bf16[128,32,32]{0,2,1:T(8,128)(2,1)} %bitcast.8), calls=%async_computation.2 | async-start | bytes 524288 | tf_op jit(solution)/shard_map/all_to_all | solution.py:137
  23.7 195.2 %reduce-scatter.2.cloned.1.call-start = ((), (), s32[]{:S(2)}) async-start(), calls=%async_computation.8 | async-start | bytes 2359296 | tf_op jit(solution)/shard_map/reduce_scatter | solution.py:121
  164.9 1.1 copy-start.8
  165.1 3.3 copy-start.12
  168.5 20.3 %all-to-all-start = ((bf16[128,32,32]{0,2,1:T(8,128)(2,1)}), bf16[128,32,32]{0,2,1:T(8,128)(2,1)S(1)}, u32[]{:S(2)}, u32[]{:S(2)}) async-start(bf16[128,32,32]{0,2,1:T(8,128)(2,1)} %bitcast.2), calls=%async_computation.1 | async-start | bytes 524288 | tf_op jit(solution)/shard_map/all_to_all | solution.py:141
  190.7 0.8 copy-start.2
  220.8 23.9 %all-to-all-start.3 = ((bf16[128,32,32]{0,2,1:T(8,128)(2,1)}), bf16[128,32,32]{0,2,1:T(8,128)(2,1)S(1)}, u32[]{:S(2)}, u32[]{:S(2)}) async-start(bf16[128,32,32]{0,2,1:T(8,128)(2,1)} %bitcast.204), calls=%async_computation.4 | async-start | bytes 524288 | tf_op jit(solution)/shard_map/all_to_all | solution.py:149
  250.3 1.2 copy-start.3
  250.3 1.5 copy-start.4
  250.4 1.8 copy-start.5
  250.4 2.1 copy-start.6
  277.0 5.9 %copy-start.7 = (f32[128,64,32]{0,1,2:T(8,128)S(1)}, f32[128,64,32]{0,1,2:T(8,128)}, u32[]{:S(2)}) copy-start(f32[128,64,32]{0,1,2:T(8,128)} %get-tuple-element.48) | copy-start | bytes 3145732
  277.0 18.7 %all-to-all-start.2 = ((bf16[32,128,32]{1,2,0:T(8,128)(2,1)}), bf16[32,128,32]{1,2,0:T(8,128)(2,1)S(1)}, u32[]{:S(2)}, u32[]{:S(2)}) async-start(bf16[32,128,32]{1,2,0:T(8,128)(2,1)} %copy.52), calls=%async_computation.3 | async-start | bytes 524288 | tf_op jit(solution)/shard_map/all_to_all | solution.py:146
  295.7 18.5 %all-to-all-start.4 = ((bf16[32,128,32]{1,2,0:T(8,128)(2,1)}), bf16[32,128,32]{1,2,0:T(8,128)(2,1)S(1)}, u32[]{:S(2)}, u32[]{:S(2)}) async-start(bf16[32,128,32]{1,2,0:T(8,128)(2,1)} %copy.61), calls=%async_computation.5 | async-start | bytes 524288 | tf_op jit(solution)/shard_map/all_to_all | solution.py:155
  299.6 96.3 %all-gather.5.cloned.1.call-start = ((), (), s32[]{:S(2)}) async-start(), calls=%async_computation.9 | async-start | bytes 3244032 | tf_op jit(solution)/shard_map/all_gather | solution.py:13
  300.7 14.0 %copy-start.11 = (bf16[128,1024]{1,0:T(8,128)(2,1)S(1)}, bf16[128,1024]{1,0:T(8,128)(2,1)}, u32[]{:S(2)}) copy-start(bf16[128,1024]{1,0:T(8,128)(2,1)} %reduce-scatter.2.cloned.1.call-done) | copy-start | bytes 786436
  314.5 1.0 copy-start.10
  314.5 1.3 copy-start.9
  325.6 19.3 %all-to-all-start.5 = ((bf16[32,128,32]{1,2,0:T(8,128)(2,1)}), bf16[32,128,32]{1,2,0:T(8,128)(2,1)S(1)}, u32[]{:S(2)}, u32[]{:S(2)}) async-start(bf16[32,128,32]{1,2,0:T(8,128)(2,1)} %copy.66), calls=%async_computation.6 | async-start | bytes 524288 | tf_op jit(solution)/shard_map/all_to_all | solution.py:156
  329.6 16.5 %copy-start.13 = (f32[1,3,1024]{2,1,0:T(4,128)S(1)}, f32[1,3,1024]{2,1,0:T(4,128)}, u32[]{:S(2)}) copy-start(f32[1,3,1024]{2,1,0:T(4,128)} %copy-done.12) | copy-start | bytes 36868
  329.6 16.4 %collective-permute-start.1 = (bf16[6,3,1024]{2,0,1:T(8,128)(2,1)S(1)}, bf16[6,3,1024]{2,0,1:T(8,128)(2,1)S(1)}, u32[]{:S(2)}, u32[]{:S(2)}) collective-permute-start(bf16[6,3,1024]{2,0,1:T(8,128)(2,1)S(1)} %slice.122), channel_id=1, source_target_pairs={{8,0},{16,8},{24,16},{32,24},{40,32},{48,40},{56,48},{64,56},{72,6... | collective-permute-start | bytes 110600 | tf_op jit(solution)/shard_map/ppermute | solution.py:24
  346.1 52.6 %copy-start.1 = (bf16[128,1024]{1,0:T(8,128)(2,1)S(1)}, bf16[128,1024]{1,0:T(8,128)(2,1)}, u32[]{:S(2)}) copy-start(bf16[128,1024]{1,0:T(8,128)(2,1)} %param.6) | copy-start | bytes 786436
Sparse Core Ops, SparseCore 0:
  10.8 141.3 all-gather.2
  165.1 53.7 reduce-scatter.1
  318.7 77.0 all-gather.4
